TPU v7x, 256 devices: a whole 4x4x8 slice. The times are simulated.
256 devices in a mesh: rows: 8 (over y_hi, x), vecs: 32 (over y_lo, z, core).
Axes of the slice: x: 4, y: 4 (y_hi: 2, y_lo: 2; y = y_hi * 2 + y_lo), z: 8, core: 2. Of those that a mesh axis runs over, the one named last changes fastest.
Arguments:
- eigvecs: float32 [16384, 4096], P('rows', 'vecs'), may hold values from -6 to 6
- reflectors: float32 [7, 8192, 256], P(None, ('rows', 'vecs')), may hold values from -6 to 6
- offsets: int32 [7, 8], P(None, 'rows'), may hold values from 0 to 1024, as said below
Outputs:
- rotated: float32 [16384, 4096], P('rows', 'vecs')
Inputs may be any that keep to these rules, and one draw needn't show every extreme that they name: `offsets`: in every tick some row block has offset 2048 - 1024 and another has offset 0.
All inputs are finite; a program needn't handle non-finite values.
Results may differ from a plain program's by a relative error of at most 0.00028.
Values sent between devices are 32-bit elements; how exact they have to be, the bound alone decides.
No kernel may reach another device: no remote copies, remote signals or barrier semaphores. Data moves between devices by JAX's collectives and lax.ppermute only.
A program may use at most 128 MiB of HBM per device.

v0:
```python
import jax
import jax.numpy as jnp
from jax import lax
from jax.experimental import pallas as pl
from jax.sharding import PartitionSpec as P

H = 256
BASE = 32


def passed_along(x, axis, by):
    size = lax.axis_size(axis)
    return lax.ppermute(x, axis, [(i, (i + by) % size) for i in range(size)])


def matmul_high(left, right):
    return jnp.matmul(left, right, precision=lax.Precision.HIGHEST, preferred_element_type=jnp.float32)


def project_onto(left, right):
    return lax.dot_general(
        left, right, (((left.ndim - 2,), (right.ndim - 2,)), ((), ())),
        precision=lax.Precision.HIGHEST, preferred_element_type=jnp.float32,
    )


def half_inverse(a, size):
    row = lax.broadcasted_iota(jnp.int32, (size, size), 0)
    col = lax.broadcasted_iota(jnp.int32, (size, size), 1)
    eye_mask = row == col
    eye = eye_mask.astype(jnp.float32)
    diag_col = jnp.sum(jnp.where(eye_mask, a, 0.0), axis=1, keepdims=True)
    diag_row = jnp.sum(jnp.where(eye_mask, a, 0.0), axis=0, keepdims=True)
    same_base = (row // BASE) == (col // BASE)
    nilpotent = jnp.where(same_base, a / diag_col, 0.0) - eye
    product = eye - nilpotent
    power = nilpotent
    span = 2
    while span < BASE:
        power = matmul_high(power, power)
        product = matmul_high(product, eye + power)
        span = span * 2
    inv = product * (1.0 / diag_row)
    half = BASE
    while half < size:
        corner_mask = ((row // half) % 2 == 0) & ((col // half) == (row // half) + 1)
        upper = jnp.where(corner_mask, a, 0.0)
        inv = inv - matmul_high(matmul_high(inv, upper), inv)
        half = half * 2
    return inv


def tri_inverse_kernel(g_ref, o_ref):
    size = g_ref.shape[0]
    half = size // 2
    row = lax.broadcasted_iota(jnp.int32, (half, half), 0)
    col = lax.broadcasted_iota(jnp.int32, (half, half), 1)

    def upper_part(x):
        return jnp.where(col > row, x, jnp.where(row == col, x * 0.5, 0.0))

    upper_inv = half_inverse(upper_part(g_ref[:half, :half]), half)
    lower_inv = half_inverse(upper_part(g_ref[half:, half:]), half)
    corner = -matmul_high(matmul_high(upper_inv, g_ref[:half, half:]), lower_inv)
    o_ref[:half, :half] = upper_inv
    o_ref[:half, half:] = corner
    o_ref[half:, :half] = jnp.zeros((half, half), jnp.float32)
    o_ref[half:, half:] = lower_inv


def tri_inverse(gram):
    return pl.pallas_call(
        tri_inverse_kernel,
        out_shape=jax.ShapeDtypeStruct(gram.shape, jnp.float32),
    )(gram)


def placed_reflector(reflector, first_row, rows_here):
    nb = reflector.shape[0]
    padded = jnp.pad(reflector, ((rows_here - nb, rows_here - nb), (0, 0)))
    return lax.dynamic_slice_in_dim(padded, rows_here - nb - first_row, rows_here, 0)


def shards(eigvecs, reflectors, offsets):
    rows_here = eigvecs.shape[0]
    ticks = reflectors.shape[0]
    gathered = lax.all_gather(reflectors, "vecs", axis=1, tiled=True)
    first_rows = offsets[:, 0]

    def prepare(step, block):
        reflector = lax.dynamic_index_in_dim(gathered, step, 0, keepdims=False)
        solve = tri_inverse(project_onto(reflector, reflector))
        placed = placed_reflector(reflector, first_rows[step], rows_here)
        own_part = lax.optimization_barrier(project_onto(placed[H:], block[: rows_here - H]))
        return placed, own_part, solve

    def finish(block, incoming, placed, own_part, solve):
        project = own_part + project_onto(placed[:H], incoming)
        weights = matmul_high(solve, project)
        return weights, jnp.concatenate([incoming, block[: rows_here - H]], axis=0)

    def tick(step, carry):
        block, incoming, placed, own_part, solve = carry
        weights, joined = finish(block, incoming, placed, own_part, solve)
        outgoing = block[rows_here - 2 * H : rows_here - H] - matmul_high(placed[rows_here - H :], weights)
        incoming = passed_along(outgoing, "rows", 1)
        block = joined - matmul_high(placed, weights)
        return (block, incoming) + prepare(step + 1, block)

    carry = (eigvecs, passed_along(eigvecs[rows_here - H :], "rows", 1)) + prepare(0, eigvecs)
    carry = lax.fori_loop(0, ticks - 1, tick, carry)
    block, incoming, placed, own_part, solve = carry
    weights, joined = finish(block, incoming, placed, own_part, solve)
    return joined - matmul_high(placed, weights)


def solution(mesh):
    in_specs = (P("rows", "vecs"), P(None, ("rows", "vecs"), None), P(None, "rows"))
    out_specs = P("rows", "vecs")
    return jax.shard_map(shards, mesh=mesh, in_specs=in_specs, out_specs=out_specs, check_vma=False)
```

profile of v0, /device:TPU:8, one launch (start us, length us, event | category | flops | bytes accessed | tf_op | source)
XLA Modules:
  0.0 275.5 jit_solution(13181352958326049744)
XLA Ops:
  12.4 70.6 %all-gather.2.cloned.1.call-done = f32[7,1024,256]{2,1,0:T(8,128)} async-done(((f32[7,32,256]{2,1,0:T(8,128)}), f32[7,1024,256]{2,1,0:T(8,128)}) %all-gather.2.cloned.1.call-update) | async-done | bytes 7340048 | tf_op jit(solution)/shard_map/all_gather | solution.py:87
  83.0 4.1 %fusion.16.g_ref = f32[256,256]{1,0:T(8,128)} fusion(f32[7,1024,256]{2,1,0:T(8,128)} %all-gather.2.cloned.1.call-done), kind=kOutput, calls=%fused_computation.26 | convolution fusion | flops 805306368 | bytes 1310720 | tf_op jit(solution)/shard_map/dot_general | solution.py:21
  87.1 4.9 %shard_map.37 = f32[256,256]{1,0:T(8,128)S(1)} custom-call(f32[256,256]{1,0:T(8,128)} %fusion.16.g_ref), custom_call_target="tpu_custom_call" | custom-call | tf_op jit(solution)/shard_map/pallas_call | solution.py:72
  94.5 3.8 %fusion.8 = f32[256,128]{1,0:T(8,128)} fusion(s32[]{:T(128)S(6)} %add.85, f32[1024,256]{1,0:T(8,128)S(1)} %slice_bitcast_fusion, f32[2048,128]{1,0:T(8,128)S(1)} %copy-done), kind=kOutput, calls=%fused_computation.17 | convolution fusion | flops 704643072 | bytes 2097156 | tf_op jit(solution)/shard_map/dot_general | solution.py:21
  98.3 162.5 %while.23 = (s32[]{:T(128)}, f32[2048,128]{0,1:T(8,128)}, f32[256,128]{0,1:T(8,128)S(1)}, f32[2048,256]{1,0:T(8,128)S(1)}, f32[256,128]{1,0:T(8,128)}, /*index=5...) while((s32[]{:T(128)}, f32[2048,128]{0,1:T(8,128)}, ...), condition=%wide.region_1.2_spmd, body=%wide.region_0.1_spmd.sunk | while | flops 2617835520 | bytes 17432864 | solution.py:111
  106.8 3.2 %fusion.59 = f32[2048,128]{0,1:T(8,128)} fusion(f32[128,256]{1,0:T(8,128)S(1)} %fusion.58, f32[2048,256]{1,0:T(8,128)S(1)} %get-tuple-element.304, f32[1792,128]{0,1:T(8,128)S(1)} %slice.109, f32[256,128]{0,1:T(8,128)S(1)} %get-tuple-element.303), kind=kOutput, calls=%fused_computation.3.clone.1 | convolution fusion | flops 805830656 | bytes 4325376 | tf_op jit(solution)/shard_map/while/body/eval_jaxpr/dot_general | solution.py:17
  114.5 5.0 %fusion.61 = f32[256,128]{1,0:T(8,128)} fusion(s32[]{:T(128)S(6)} %add.98, f32[1024,256]{1,0:T(8,128)S(1)} %dynamic-slice_bitcast_fusion.2, f32[2048,128]{0,1:T(8,128)} %fusion.59), kind=kOutput, calls=%fused_computation.4.clone.1 | convolution fusion | flops 704643072 | bytes 2097156 | tf_op jit(solution)/shard_map/while/body/eval_jaxpr/dot_general | solution.py:21
  119.5 4.9 %eval_jaxpr.8 = f32[256,256]{1,0:T(8,128)S(1)} custom-call(f32[256,256]{1,0:T(8,128)} %fusion.62.g_ref), custom_call_target="tpu_custom_call" | custom-call | tf_op jit(solution)/shard_map/while/body/eval_jaxpr/pallas_call | solution.py:72
  133.8 3.2 %fusion.59 = f32[2048,128]{0,1:T(8,128)} fusion(f32[128,256]{1,0:T(8,128)S(1)} %fusion.58, f32[2048,256]{1,0:T(8,128)S(1)} %get-tuple-element.304, f32[1792,128]{0,1:T(8,128)S(1)} %slice.109, f32[256,128]{0,1:T(8,128)S(1)} %get-tuple-element.303), kind=kOutput, calls=%fused_computation.3.clone.1 | convolution fusion | flops 805830656 | bytes 4325376 | tf_op jit(solution)/shard_map/while/body/eval_jaxpr/dot_general | solution.py:17
  141.6 5.0 %fusion.61 = f32[256,128]{1,0:T(8,128)} fusion(s32[]{:T(128)S(6)} %add.98, f32[1024,256]{1,0:T(8,128)S(1)} %dynamic-slice_bitcast_fusion.2, f32[2048,128]{0,1:T(8,128)} %fusion.59), kind=kOutput, calls=%fused_computation.4.clone.1 | convolution fusion | flops 704643072 | bytes 2097156 | tf_op jit(solution)/shard_map/while/body/eval_jaxpr/dot_general | solution.py:21
  146.5 4.9 %eval_jaxpr.8 = f32[256,256]{1,0:T(8,128)S(1)} custom-call(f32[256,256]{1,0:T(8,128)} %fusion.62.g_ref), custom_call_target="tpu_custom_call" | custom-call | tf_op jit(solution)/shard_map/while/body/eval_jaxpr/pallas_call | solution.py:72
  160.6 3.2 %fusion.59 = f32[2048,128]{0,1:T(8,128)} fusion(f32[128,256]{1,0:T(8,128)S(1)} %fusion.58, f32[2048,256]{1,0:T(8,128)S(1)} %get-tuple-element.304, f32[1792,128]{0,1:T(8,128)S(1)} %slice.109, f32[256,128]{0,1:T(8,128)S(1)} %get-tuple-element.303), kind=kOutput, calls=%fused_computation.3.clone.1 | convolution fusion | flops 805830656 | bytes 4325376 | tf_op jit(solution)/shard_map/while/body/eval_jaxpr/dot_general | solution.py:17
  168.3 5.0 %fusion.61 = f32[256,128]{1,0:T(8,128)} fusion(s32[]{:T(128)S(6)} %add.98, f32[1024,256]{1,0:T(8,128)S(1)} %dynamic-slice_bitcast_fusion.2, f32[2048,128]{0,1:T(8,128)} %fusion.59), kind=kOutput, calls=%fused_computation.4.clone.1 | convolution fusion | flops 704643072 | bytes 2097156 | tf_op jit(solution)/shard_map/while/body/eval_jaxpr/dot_general | solution.py:21
  173.3 4.9 %eval_jaxpr.8 = f32[256,256]{1,0:T(8,128)S(1)} custom-call(f32[256,256]{1,0:T(8,128)} %fusion.62.g_ref), custom_call_target="tpu_custom_call" | custom-call | tf_op jit(solution)/shard_map/while/body/eval_jaxpr/pallas_call | solution.py:72
  188.2 3.2 %fusion.59 = f32[2048,128]{0,1:T(8,128)} fusion(f32[128,256]{1,0:T(8,128)S(1)} %fusion.58, f32[2048,256]{1,0:T(8,128)S(1)} %get-tuple-element.304, f32[1792,128]{0,1:T(8,128)S(1)} %slice.109, f32[256,128]{0,1:T(8,128)S(1)} %get-tuple-element.303), kind=kOutput, calls=%fused_computation.3.clone.1 | convolution fusion | flops 805830656 | bytes 4325376 | tf_op jit(solution)/shard_map/while/body/eval_jaxpr/dot_general | solution.py:17
  195.9 5.0 %fusion.61 = f32[256,128]{1,0:T(8,128)} fusion(s32[]{:T(128)S(6)} %add.98, f32[1024,256]{1,0:T(8,128)S(1)} %dynamic-slice_bitcast_fusion.2, f32[2048,128]{0,1:T(8,128)} %fusion.59), kind=kOutput, calls=%fused_computation.4.clone.1 | convolution fusion | flops 704643072 | bytes 2097156 | tf_op jit(solution)/shard_map/while/body/eval_jaxpr/dot_general | solution.py:21
  200.9 4.9 %eval_jaxpr.8 = f32[256,256]{1,0:T(8,128)S(1)} custom-call(f32[256,256]{1,0:T(8,128)} %fusion.62.g_ref), custom_call_target="tpu_custom_call" | custom-call | tf_op jit(solution)/shard_map/while/body/eval_jaxpr/pallas_call | solution.py:72
  215.3 3.2 %fusion.59 = f32[2048,128]{0,1:T(8,128)} fusion(f32[128,256]{1,0:T(8,128)S(1)} %fusion.58, f32[2048,256]{1,0:T(8,128)S(1)} %get-tuple-element.304, f32[1792,128]{0,1:T(8,128)S(1)} %slice.109, f32[256,128]{0,1:T(8,128)S(1)} %get-tuple-element.303), kind=kOutput, calls=%fused_computation.3.clone.1 | convolution fusion | flops 805830656 | bytes 4325376 | tf_op jit(solution)/shard_map/while/body/eval_jaxpr/dot_general | solution.py:17
  223.0 5.0 %fusion.61 = f32[256,128]{1,0:T(8,128)} fusion(s32[]{:T(128)S(6)} %add.98, f32[1024,256]{1,0:T(8,128)S(1)} %dynamic-slice_bitcast_fusion.2, f32[2048,128]{0,1:T(8,128)} %fusion.59), kind=kOutput, calls=%fused_computation.4.clone.1 | convolution fusion | flops 704643072 | bytes 2097156 | tf_op jit(solution)/shard_map/while/body/eval_jaxpr/dot_general | solution.py:21
  227.9 4.9 %eval_jaxpr.8 = f32[256,256]{1,0:T(8,128)S(1)} custom-call(f32[256,256]{1,0:T(8,128)} %fusion.62.g_ref), custom_call_target="tpu_custom_call" | custom-call | tf_op jit(solution)/shard_map/while/body/eval_jaxpr/pallas_call | solution.py:72
  242.3 3.2 %fusion.59 = f32[2048,128]{0,1:T(8,128)} fusion(f32[128,256]{1,0:T(8,128)S(1)} %fusion.58, f32[2048,256]{1,0:T(8,128)S(1)} %get-tuple-element.304, f32[1792,128]{0,1:T(8,128)S(1)} %slice.109, f32[256,128]{0,1:T(8,128)S(1)} %get-tuple-element.303), kind=kOutput, calls=%fused_computation.3.clone.1 | convolution fusion | flops 805830656 | bytes 4325376 | tf_op jit(solution)/shard_map/while/body/eval_jaxpr/dot_general | solution.py:17
  250.0 5.0 %fusion.61 = f32[256,128]{1,0:T(8,128)} fusion(s32[]{:T(128)S(6)} %add.98, f32[1024,256]{1,0:T(8,128)S(1)} %dynamic-slice_bitcast_fusion.2, f32[2048,128]{0,1:T(8,128)} %fusion.59), kind=kOutput, calls=%fused_computation.4.clone.1 | convolution fusion | flops 704643072 | bytes 2097156 | tf_op jit(solution)/shard_map/while/body/eval_jaxpr/dot_general | solution.py:21
  255.0 4.9 %eval_jaxpr.8 = f32[256,256]{1,0:T(8,128)S(1)} custom-call(f32[256,256]{1,0:T(8,128)} %fusion.62.g_ref), custom_call_target="tpu_custom_call" | custom-call | tf_op jit(solution)/shard_map/while/body/eval_jaxpr/pallas_call | solution.py:72
  265.9 2.8 %convolution_subtract_fusion = f32[2048,128]{1,0:T(8,128)} fusion(f32[2048,256]{1,0:T(8,128)S(1)} %get-tuple-element.211, f32[256,128]{1,0:T(8,128)S(1)} %fusion.12, f32[1792,128]{1,0:T(8,128)S(1)} %slice.88, f32[256,128]{1,0:T(8,128)S(1)} %copy-done.1), kind=kOutput, calls=%fused_computation.16 | convolution fusion | flops 805830656 | bytes 4325376 | tf_op jit(solution)/shard_map/dot_general | solution.py:17
  (85 shorter events, 88.8 us)
Async XLA Ops:
  6.5 5.7 %copy-start.2 = (s32[7,1]{0,1:T(1,128)S(1)}, s32[7,1]{0,1:T(1,128)}, u32[]{:S(2)}) copy-start(s32[7,1]{0,1:T(1,128)} %param.7) | copy-start | bytes 88
  6.5 76.4 %all-gather.2.cloned.1.call-start = ((), (), s32[]{:S(2)}) async-start(), calls=%async_computation | async-start | bytes 7569408 | tf_op jit(solution)/shard_map/all_gather | solution.py:87
  10.7 87.6 %collective-permute-start.1 = (f32[256,128]{0,1:T(8,128)S(1)}, f32[256,128]{0,1:T(8,128)S(1)}, u32[]{:S(2)}, u32[]{:S(2)}) collective-permute-start(f32[256,128]{0,1:T(8,128)S(1)} %slice.87), channel_id=1, source_target_pairs={{0,32},{32,64},{64,96},{96,128},{128,160},{160,192},{192,224},{224... | collective-permute-start | bytes 393224 | tf_op jit(solution)/shard_map/ppermute | solution.py:13
  93.3 1.2 copy-start
  102.2 22.2 %collective-permute-start = (f32[256,128]{0,1:T(8,128)}, f32[256,128]{0,1:T(8,128)}, u32[]{:S(2)}, u32[]{:S(2)}) collective-permute-start(f32[256,128]{0,1:T(8,128)} %fusion.60), channel_id=1, source_target_pairs={{0,32},{32,64},{64,96},{96,128},{128,160},{160,192},{192,224},{224... | collective-permute-start | bytes 393224 | tf_op jit(solution)/shard_map/while/body/eval_jaxpr/ppermute | solution.py:13
  129.2 22.3 %collective-permute-start = (f32[256,128]{0,1:T(8,128)}, f32[256,128]{0,1:T(8,128)}, u32[]{:S(2)}, u32[]{:S(2)}) collective-permute-start(f32[256,128]{0,1:T(8,128)} %fusion.60), channel_id=1, source_target_pairs={{0,32},{32,64},{64,96},{96,128},{128,160},{160,192},{192,224},{224... | collective-permute-start | bytes 393224 | tf_op jit(solution)/shard_map/while/body/eval_jaxpr/ppermute | solution.py:13
  156.3 22.0 %collective-permute-start = (f32[256,128]{0,1:T(8,128)}, f32[256,128]{0,1:T(8,128)}, u32[]{:S(2)}, u32[]{:S(2)}) collective-permute-start(f32[256,128]{0,1:T(8,128)} %fusion.60), channel_id=1, source_target_pairs={{0,32},{32,64},{64,96},{96,128},{128,160},{160,192},{192,224},{224... | collective-permute-start | bytes 393224 | tf_op jit(solution)/shard_map/while/body/eval_jaxpr/ppermute | solution.py:13
  183.0 22.9 %collective-permute-start = (f32[256,128]{0,1:T(8,128)}, f32[256,128]{0,1:T(8,128)}, u32[]{:S(2)}, u32[]{:S(2)}) collective-permute-start(f32[256,128]{0,1:T(8,128)} %fusion.60), channel_id=1, source_target_pairs={{0,32},{32,64},{64,96},{96,128},{128,160},{160,192},{192,224},{224... | collective-permute-start | bytes 393224 | tf_op jit(solution)/shard_map/while/body/eval_jaxpr/ppermute | solution.py:13
  210.6 22.3 %collective-permute-start = (f32[256,128]{0,1:T(8,128)}, f32[256,128]{0,1:T(8,128)}, u32[]{:S(2)}, u32[]{:S(2)}) collective-permute-start(f32[256,128]{0,1:T(8,128)} %fusion.60), channel_id=1, source_target_pairs={{0,32},{32,64},{64,96},{96,128},{128,160},{160,192},{192,224},{224... | collective-permute-start | bytes 393224 | tf_op jit(solution)/shard_map/while/body/eval_jaxpr/ppermute | solution.py:13
  237.7 22.3 %collective-permute-start = (f32[256,128]{0,1:T(8,128)}, f32[256,128]{0,1:T(8,128)}, u32[]{:S(2)}, u32[]{:S(2)}) collective-permute-start(f32[256,128]{0,1:T(8,128)} %fusion.60), channel_id=1, source_target_pairs={{0,32},{32,64},{64,96},{96,128},{128,160},{160,192},{192,224},{224... | collective-permute-start | bytes 393224 | tf_op jit(solution)/shard_map/while/body/eval_jaxpr/ppermute | solution.py:13
  264.4 1.4 copy-start.1
Sparse Core Ops, SparseCore 0:
  9.2 73.7 all-gather.1
where the time goes:
time: 278 us; the launch traced here: 276 us
  matrix products  101 us (36%)
  waiting for transfers between devices  71.4 us (26%)
  local copies, waits for them, and re-layouts  36.4 us (13%)
  Pallas kernels  34.6 us (12%)
  between operations  13.5 us (5%)
  starting transfers between devices  10.7 us (4%)
  loops' own time  8.1 us (3%)
    all_gather x1, waiting for transfers between devices, shards(): gathered = lax.all_gather(reflectors, 'vecs', axis=1, tiled=True)  70.6 us
    dot_general x21, matrix products, project_onto(): lax.dot_general(left, right, (((left.ndim - 2,), (right.ndim - 2,)), ((),...  63.1 us
    dot_general x20, matrix products, matmul_high(): jnp.matmul(left, right, precision=lax.Precision.HIGHEST, preferred_elemen...  37.6 us
    pallas_call x7, Pallas kernels, tri_inverse(): pl.pallas_call(tri_inverse_kernel, out_shape=jax.ShapeDtypeStruct(gram.sh...  34.6 us
    ppermute x7, starting transfers between devices, passed_along(): return lax.ppermute(x, axis, [(i, (i + by) % size) for i in range(size)])  10.7 us
    squeeze x7, local copies, waits for them, and re-layouts, prepare(): reflector = lax.dynamic_index_in_dim(gathered, step, 0, keepdims=False)  9.05 us
    another operation x1, loops' own time, shards(): carry = lax.fori_loop(0, ticks - 1, tick, carry)  8.1 us
    slice x7, local copies, waits for them, and re-layouts, finish(): return (weights, jnp.concatenate([incoming, block[:rows_here - H]], axis=0))  7.49 us
  transfers between devices with their start and end apart: 8, of which 1 were waited for; matrix products, arithmetic and copies ran while one was open for 36% of the time, Pallas kernels for 13%

commit v1 on v0

--- a/solution.py
+++ b/solution.py
@@ -17,10 +17,14 @@
     return jnp.matmul(left, right, precision=lax.Precision.HIGHEST, preferred_element_type=jnp.float32)
 
 
+def matmul_3x(left, right):
+    return jnp.matmul(left, right, precision=lax.Precision.HIGH, preferred_element_type=jnp.float32)
+
+
 def project_onto(left, right):
     return lax.dot_general(
         left, right, (((left.ndim - 2,), (right.ndim - 2,)), ((), ())),
-        precision=lax.Precision.HIGHEST, preferred_element_type=jnp.float32,
+        precision=lax.Precision.HIGH, preferred_element_type=jnp.float32,
     )
 
 
@@ -96,22 +100,22 @@
 
     def finish(block, incoming, placed, own_part, solve):
         project = own_part + project_onto(placed[:H], incoming)
-        weights = matmul_high(solve, project)
+        weights = matmul_3x(solve, project)
         return weights, jnp.concatenate([incoming, block[: rows_here - H]], axis=0)
 
     def tick(step, carry):
         block, incoming, placed, own_part, solve = carry
         weights, joined = finish(block, incoming, placed, own_part, solve)
-        outgoing = block[rows_here - 2 * H : rows_here - H] - matmul_high(placed[rows_here - H :], weights)
+        outgoing = block[rows_here - 2 * H : rows_here - H] - matmul_3x(placed[rows_here - H :], weights)
         incoming = passed_along(outgoing, "rows", 1)
-        block = joined - matmul_high(placed, weights)
+        block = joined - matmul_3x(placed, weights)
         return (block, incoming) + prepare(step + 1, block)
 
     carry = (eigvecs, passed_along(eigvecs[rows_here - H :], "rows", 1)) + prepare(0, eigvecs)
     carry = lax.fori_loop(0, ticks - 1, tick, carry)
     block, incoming, placed, own_part, solve = carry
     weights, joined = finish(block, incoming, placed, own_part, solve)
-    return joined - matmul_high(placed, weights)
+    return joined - matmul_3x(placed, weights)
 
 
 def solution(mesh):

time: 278 us -> 251 us (0.903)
  matrix products: 101 us -> 74.3 us
    dot_general x21, matrix products: 63.1 us -> 45.3 us  [project_onto(): lax.dot_general(left, right, (((left.ndim - 2,), (right.ndim - 2,)), ((),...]
    dot_general x20, matrix products: 37.6 us -> 29 us  [matmul_3x(): jnp.matmul(left, right, precision=lax.Precision.HIGH, preferred_element_t...]
  transfers between devices with their start and end apart: 8 -> 8, of which waited for: 1 -> 1; matrix products, arithmetic and copies ran while one was open for 36% -> 31% of each run, Pallas kernels for 13% -> 14%
where the time goes in v1:
time: 251 us; the launch traced here: 249 us
  matrix products  74.3 us (30%)
  waiting for transfers between devices  71.4 us (28%)
  local copies, waits for them, and re-layouts  36.5 us (15%)
  Pallas kernels  34.6 us (14%)
  between operations  13.5 us (5%)
  starting transfers between devices  10.7 us (4%)
  loops' own time  8.1 us (3%)
    all_gather x1, waiting for transfers between devices, shards(): gathered = lax.all_gather(reflectors, 'vecs', axis=1, tiled=True)  70.6 us
    dot_general x21, matrix products, project_onto(): lax.dot_general(left, right, (((left.ndim - 2,), (right.ndim - 2,)), ((),...  45.3 us
    pallas_call x7, Pallas kernels, tri_inverse(): pl.pallas_call(tri_inverse_kernel, out_shape=jax.ShapeDtypeStruct(gram.sh...  34.6 us
    dot_general x20, matrix products, matmul_3x(): jnp.matmul(left, right, precision=lax.Precision.HIGH, preferred_element_t...  29 us
    ppermute x7, starting transfers between devices, passed_along(): return lax.ppermute(x, axis, [(i, (i + by) % size) for i in range(size)])  10.7 us
    squeeze x7, local copies, waits for them, and re-layouts, prepare(): reflector = lax.dynamic_index_in_dim(gathered, step, 0, keepdims=False)  9.05 us
    another operation x1, loops' own time, shards(): carry = lax.fori_loop(0, ticks - 1, tick, carry)  8.1 us
    slice x7, local copies, waits for them, and re-layouts, finish(): return (weights, jnp.concatenate([incoming, block[:rows_here - H]], axis=0))  7.49 us
  transfers between devices with their start and end apart: 8, of which 1 were waited for; matrix products, arithmetic and copies ran while one was open for 31% of the time, Pallas kernels for 14%

profile of v1, /device:TPU:8, one launch (start us, length us, event | category | flops | bytes accessed | tf_op | source)
XLA Modules:
  0.0 249.0 jit_solution(2219730295153886005)
XLA Ops:
  7.3 2.5 %copy.5 = f32[2048,128]{0,1:T(8,128)} copy(f32[2048,128]{1,0:T(8,128)} %param.5) | data formatting | bytes 2097152 | tf_op jit(solution)/shard_map/while | solution.py:115
  12.4 70.6 %all-gather.2.cloned.1.call-done = f32[7,1024,256]{2,1,0:T(8,128)} async-done(((f32[7,32,256]{2,1,0:T(8,128)}), f32[7,1024,256]{2,1,0:T(8,128)}) %all-gather.2.cloned.1.call-update) | async-done | bytes 7340048 | tf_op jit(solution)/shard_map/all_gather | solution.py:91
  83.0 3.2 %fusion.16.g_ref = f32[256,256]{1,0:T(8,128)} fusion(f32[7,1024,256]{2,1,0:T(8,128)} %all-gather.2.cloned.1.call-done), kind=kOutput, calls=%fused_computation.26 | convolution fusion | flops 402653184 | bytes 1310720 | tf_op jit(solution)/shard_map/dot_general | solution.py:25
  86.2 4.9 %shard_map.37 = f32[256,256]{1,0:T(8,128)S(1)} custom-call(f32[256,256]{1,0:T(8,128)} %fusion.16.g_ref), custom_call_target="tpu_custom_call" | custom-call | tf_op jit(solution)/shard_map/pallas_call | solution.py:76
  93.7 2.3 fusion.8
  96.0 139.5 %while.23 = (s32[]{:T(128)}, f32[2048,128]{0,1:T(8,128)}, f32[256,128]{0,1:T(8,128)S(1)}, f32[2048,256]{1,0:T(8,128)S(1)}, f32[256,128]{1,0:T(8,128)}, /*index=5...) while((s32[]{:T(128)}, f32[2048,128]{0,1:T(8,128)}, ...), condition=%wide.region_1.2_spmd, body=%wide.region_0.1_spmd.sunk | while | flops 1309212672 | bytes 17432864 | solution.py:115
  104.1 2.1 fusion.59
  109.9 3.5 %fusion.61 = f32[256,128]{1,0:T(8,128)} fusion(s32[]{:T(128)S(6)} %add.98, f32[1024,256]{1,0:T(8,128)S(1)} %dynamic-slice_bitcast_fusion.2, f32[2048,128]{0,1:T(8,128)} %fusion.59), kind=kOutput, calls=%fused_computation.4.clone.1 | convolution fusion | flops 352321536 | bytes 2097156 | tf_op jit(solution)/shard_map/while/body/eval_jaxpr/dot_general | solution.py:25
  113.4 4.9 %eval_jaxpr.8 = f32[256,256]{1,0:T(8,128)S(1)} custom-call(f32[256,256]{1,0:T(8,128)} %fusion.62.g_ref), custom_call_target="tpu_custom_call" | custom-call | tf_op jit(solution)/shard_map/while/body/eval_jaxpr/pallas_call | solution.py:76
  127.3 2.1 fusion.59
  133.1 3.5 %fusion.61 = f32[256,128]{1,0:T(8,128)} fusion(s32[]{:T(128)S(6)} %add.98, f32[1024,256]{1,0:T(8,128)S(1)} %dynamic-slice_bitcast_fusion.2, f32[2048,128]{0,1:T(8,128)} %fusion.59), kind=kOutput, calls=%fused_computation.4.clone.1 | convolution fusion | flops 352321536 | bytes 2097156 | tf_op jit(solution)/shard_map/while/body/eval_jaxpr/dot_general | solution.py:25
  136.5 4.9 %eval_jaxpr.8 = f32[256,256]{1,0:T(8,128)S(1)} custom-call(f32[256,256]{1,0:T(8,128)} %fusion.62.g_ref), custom_call_target="tpu_custom_call" | custom-call | tf_op jit(solution)/shard_map/while/body/eval_jaxpr/pallas_call | solution.py:76
  150.2 2.1 fusion.59
  156.0 3.5 %fusion.61 = f32[256,128]{1,0:T(8,128)} fusion(s32[]{:T(128)S(6)} %add.98, f32[1024,256]{1,0:T(8,128)S(1)} %dynamic-slice_bitcast_fusion.2, f32[2048,128]{0,1:T(8,128)} %fusion.59), kind=kOutput, calls=%fused_computation.4.clone.1 | convolution fusion | flops 352321536 | bytes 2097156 | tf_op jit(solution)/shard_map/while/body/eval_jaxpr/dot_general | solution.py:25
  159.5 4.9 %eval_jaxpr.8 = f32[256,256]{1,0:T(8,128)S(1)} custom-call(f32[256,256]{1,0:T(8,128)} %fusion.62.g_ref), custom_call_target="tpu_custom_call" | custom-call | tf_op jit(solution)/shard_map/while/body/eval_jaxpr/pallas_call | solution.py:76
  174.0 2.1 fusion.59
  179.8 3.5 %fusion.61 = f32[256,128]{1,0:T(8,128)} fusion(s32[]{:T(128)S(6)} %add.98, f32[1024,256]{1,0:T(8,128)S(1)} %dynamic-slice_bitcast_fusion.2, f32[2048,128]{0,1:T(8,128)} %fusion.59), kind=kOutput, calls=%fused_computation.4.clone.1 | convolution fusion | flops 352321536 | bytes 2097156 | tf_op jit(solution)/shard_map/while/body/eval_jaxpr/dot_general | solution.py:25
  183.3 4.9 %eval_jaxpr.8 = f32[256,256]{1,0:T(8,128)S(1)} custom-call(f32[256,256]{1,0:T(8,128)} %fusion.62.g_ref), custom_call_target="tpu_custom_call" | custom-call | tf_op jit(solution)/shard_map/while/body/eval_jaxpr/pallas_call | solution.py:76
  197.2 2.1 fusion.59
  203.0 3.5 %fusion.61 = f32[256,128]{1,0:T(8,128)} fusion(s32[]{:T(128)S(6)} %add.98, f32[1024,256]{1,0:T(8,128)S(1)} %dynamic-slice_bitcast_fusion.2, f32[2048,128]{0,1:T(8,128)} %fusion.59), kind=kOutput, calls=%fused_computation.4.clone.1 | convolution fusion | flops 352321536 | bytes 2097156 | tf_op jit(solution)/shard_map/while/body/eval_jaxpr/dot_general | solution.py:25
  206.5 4.9 %eval_jaxpr.8 = f32[256,256]{1,0:T(8,128)S(1)} custom-call(f32[256,256]{1,0:T(8,128)} %fusion.62.g_ref), custom_call_target="tpu_custom_call" | custom-call | tf_op jit(solution)/shard_map/while/body/eval_jaxpr/pallas_call | solution.py:76
  220.3 2.1 fusion.59
  226.1 3.5 %fusion.61 = f32[256,128]{1,0:T(8,128)} fusion(s32[]{:T(128)S(6)} %add.98, f32[1024,256]{1,0:T(8,128)S(1)} %dynamic-slice_bitcast_fusion.2, f32[2048,128]{0,1:T(8,128)} %fusion.59), kind=kOutput, calls=%fused_computation.4.clone.1 | convolution fusion | flops 352321536 | bytes 2097156 | tf_op jit(solution)/shard_map/while/body/eval_jaxpr/dot_general | solution.py:25
  229.6 4.9 %eval_jaxpr.8 = f32[256,256]{1,0:T(8,128)S(1)} custom-call(f32[256,256]{1,0:T(8,128)} %fusion.62.g_ref), custom_call_target="tpu_custom_call" | custom-call | tf_op jit(solution)/shard_map/while/body/eval_jaxpr/pallas_call | solution.py:76
  (85 shorter events, 80.4 us)
Async XLA Ops:
  6.5 5.7 %copy-start.2 = (s32[7,1]{0,1:T(1,128)S(1)}, s32[7,1]{0,1:T(1,128)}, u32[]{:S(2)}) copy-start(s32[7,1]{0,1:T(1,128)} %param.7) | copy-start | bytes 88
  6.5 76.4 %all-gather.2.cloned.1.call-start = ((), (), s32[]{:S(2)}) async-start(), calls=%async_computation | async-start | bytes 7569408 | tf_op jit(solution)/shard_map/all_gather | solution.py:91
  10.7 85.3 %collective-permute-start.1 = (f32[256,128]{0,1:T(8,128)S(1)}, f32[256,128]{0,1:T(8,128)S(1)}, u32[]{:S(2)}, u32[]{:S(2)}) collective-permute-start(f32[256,128]{0,1:T(8,128)S(1)} %slice.87), channel_id=1, source_target_pairs={{0,32},{32,64},{64,96},{96,128},{128,160},{160,192},{192,224},{224... | collective-permute-start | bytes 393224 | tf_op jit(solution)/shard_map/ppermute | solution.py:13
  92.5 1.2 copy-start
  99.5 18.9 %collective-permute-start = (f32[256,128]{0,1:T(8,128)}, f32[256,128]{0,1:T(8,128)}, u32[]{:S(2)}, u32[]{:S(2)}) collective-permute-start(f32[256,128]{0,1:T(8,128)} %fusion.60), channel_id=1, source_target_pairs={{0,32},{32,64},{64,96},{96,128},{128,160},{160,192},{192,224},{224... | collective-permute-start | bytes 393224 | tf_op jit(solution)/shard_map/while/body/eval_jaxpr/ppermute | solution.py:13
  122.7 18.8 %collective-permute-start = (f32[256,128]{0,1:T(8,128)}, f32[256,128]{0,1:T(8,128)}, u32[]{:S(2)}, u32[]{:S(2)}) collective-permute-start(f32[256,128]{0,1:T(8,128)} %fusion.60), channel_id=1, source_target_pairs={{0,32},{32,64},{64,96},{96,128},{128,160},{160,192},{192,224},{224... | collective-permute-start | bytes 393224 | tf_op jit(solution)/shard_map/while/body/eval_jaxpr/ppermute | solution.py:13
  145.8 18.6 %collective-permute-start = (f32[256,128]{0,1:T(8,128)}, f32[256,128]{0,1:T(8,128)}, u32[]{:S(2)}, u32[]{:S(2)}) collective-permute-start(f32[256,128]{0,1:T(8,128)} %fusion.60), channel_id=1, source_target_pairs={{0,32},{32,64},{64,96},{96,128},{128,160},{160,192},{192,224},{224... | collective-permute-start | bytes 393224 | tf_op jit(solution)/shard_map/while/body/eval_jaxpr/ppermute | solution.py:13
  168.8 19.4 %collective-permute-start = (f32[256,128]{0,1:T(8,128)}, f32[256,128]{0,1:T(8,128)}, u32[]{:S(2)}, u32[]{:S(2)}) collective-permute-start(f32[256,128]{0,1:T(8,128)} %fusion.60), channel_id=1, source_target_pairs={{0,32},{32,64},{64,96},{96,128},{128,160},{160,192},{192,224},{224... | collective-permute-start | bytes 393224 | tf_op jit(solution)/shard_map/while/body/eval_jaxpr/ppermute | solution.py:13
  192.6 18.8 %collective-permute-start = (f32[256,128]{0,1:T(8,128)}, f32[256,128]{0,1:T(8,128)}, u32[]{:S(2)}, u32[]{:S(2)}) collective-permute-start(f32[256,128]{0,1:T(8,128)} %fusion.60), channel_id=1, source_target_pairs={{0,32},{32,64},{64,96},{96,128},{128,160},{160,192},{192,224},{224... | collective-permute-start | bytes 393224 | tf_op jit(solution)/shard_map/while/body/eval_jaxpr/ppermute | solution.py:13
  215.8 18.8 %collective-permute-start = (f32[256,128]{0,1:T(8,128)}, f32[256,128]{0,1:T(8,128)}, u32[]{:S(2)}, u32[]{:S(2)}) collective-permute-start(f32[256,128]{0,1:T(8,128)} %fusion.60), channel_id=1, source_target_pairs={{0,32},{32,64},{64,96},{96,128},{128,160},{160,192},{192,224},{224... | collective-permute-start | bytes 393224 | tf_op jit(solution)/shard_map/while/body/eval_jaxpr/ppermute | solution.py:13
  238.8 1.3 copy-start.1
Sparse Core Ops, SparseCore 0:
  9.2 73.7 all-gather.1

commit v2 on v1

--- a/solution.py
+++ b/solution.py
@@ -11,10 +11,6 @@
 def passed_along(x, axis, by):
     size = lax.axis_size(axis)
     return lax.ppermute(x, axis, [(i, (i + by) % size) for i in range(size)])
-
-
-def matmul_high(left, right):
-    return jnp.matmul(left, right, precision=lax.Precision.HIGHEST, preferred_element_type=jnp.float32)
 
 
 def matmul_3x(left, right):
@@ -41,15 +37,15 @@
     power = nilpotent
     span = 2
     while span < BASE:
-        power = matmul_high(power, power)
-        product = matmul_high(product, eye + power)
+        power = matmul_3x(power, power)
+        product = matmul_3x(product, eye + power)
         span = span * 2
     inv = product * (1.0 / diag_row)
     half = BASE
     while half < size:
         corner_mask = ((row // half) % 2 == 0) & ((col // half) == (row // half) + 1)
         upper = jnp.where(corner_mask, a, 0.0)
-        inv = inv - matmul_high(matmul_high(inv, upper), inv)
+        inv = inv - matmul_3x(matmul_3x(inv, upper), inv)
         half = half * 2
     return inv
 
@@ -65,7 +61,7 @@
 
     upper_inv = half_inverse(upper_part(g_ref[:half, :half]), half)
     lower_inv = half_inverse(upper_part(g_ref[half:, half:]), half)
-    corner = -matmul_high(matmul_high(upper_inv, g_ref[:half, half:]), lower_inv)
+    corner = -matmul_3x(matmul_3x(upper_inv, g_ref[:half, half:]), lower_inv)
     o_ref[:half, :half] = upper_inv
     o_ref[:half, half:] = corner
     o_ref[half:, :half] = jnp.zeros((half, half), jnp.float32)

time: 251 us -> 245 us (0.976)
  Pallas kernels: 34.6 us -> 27.7 us
    pallas_call x7, Pallas kernels: 34.6 us -> 27.7 us  [tri_inverse(): pl.pallas_call(tri_inverse_kernel, out_shape=jax.ShapeDtypeStruct(gram.sh...]
  transfers between devices with their start and end apart: 8 -> 8, of which waited for: 1 -> 1; matrix products, arithmetic and copies ran while one was open for 31% -> 32% of each run, Pallas kernels for 14% -> 11%
where the time goes in v2:
time: 245 us; the launch traced here: 242 us
  matrix products  74.3 us (30%)
  waiting for transfers between devices  71.4 us (29%)
  local copies, waits for them, and re-layouts  36.5 us (15%)
  Pallas kernels  27.7 us (11%)
  between operations  13.5 us (6%)
  starting transfers between devices  10.7 us (4%)
  loops' own time  8.1 us (3%)
    all_gather x1, waiting for transfers between devices, shards(): gathered = lax.all_gather(reflectors, 'vecs', axis=1, tiled=True)  70.6 us
    dot_general x21, matrix products, project_onto(): lax.dot_general(left, right, (((left.ndim - 2,), (right.ndim - 2,)), ((),...  45.3 us
    dot_general x20, matrix products, matmul_3x(): jnp.matmul(left, right, precision=lax.Precision.HIGH, preferred_element_t...  29 us
    pallas_call x7, Pallas kernels, tri_inverse(): pl.pallas_call(tri_inverse_kernel, out_shape=jax.ShapeDtypeStruct(gram.sh...  27.7 us
    ppermute x7, starting transfers between devices, passed_along(): return lax.ppermute(x, axis, [(i, (i + by) % size) for i in range(size)])  10.7 us
    squeeze x7, local copies, waits for them, and re-layouts, prepare(): reflector = lax.dynamic_index_in_dim(gathered, step, 0, keepdims=False)  9.05 us
    another operation x1, loops' own time, shards(): carry = lax.fori_loop(0, ticks - 1, tick, carry)  8.1 us
    slice x7, local copies, waits for them, and re-layouts, finish(): return (weights, jnp.concatenate([incoming, block[:rows_here - H]], axis=0))  7.49 us
  transfers between devices with their start and end apart: 8, of which 1 were waited for; matrix products, arithmetic and copies ran while one was open for 32% of the time, Pallas kernels for 11%

profile of v2, /device:TPU:8, one launch (start us, length us, event | category | flops | bytes accessed | tf_op | source)
XLA Modules:
  0.0 242.2 jit_solution(13479740385416189345)
XLA Ops:
  7.3 2.5 %copy.5 = f32[2048,128]{0,1:T(8,128)} copy(f32[2048,128]{1,0:T(8,128)} %param.5) | data formatting | bytes 2097152 | tf_op jit(solution)/shard_map/while | solution.py:111
  12.4 70.6 %all-gather.2.cloned.1.call-done = f32[7,1024,256]{2,1,0:T(8,128)} async-done(((f32[7,32,256]{2,1,0:T(8,128)}), f32[7,1024,256]{2,1,0:T(8,128)}) %all-gather.2.cloned.1.call-update) | async-done | bytes 7340048 | tf_op jit(solution)/shard_map/all_gather | solution.py:87
  83.0 3.2 %fusion.16.g_ref = f32[256,256]{1,0:T(8,128)} fusion(f32[7,1024,256]{2,1,0:T(8,128)} %all-gather.2.cloned.1.call-done), kind=kOutput, calls=%fused_computation.26 | convolution fusion | flops 402653184 | bytes 1310720 | tf_op jit(solution)/shard_map/dot_general | solution.py:21
  86.2 4.0 %shard_map.37 = f32[256,256]{1,0:T(8,128)S(1)} custom-call(f32[256,256]{1,0:T(8,128)} %fusion.16.g_ref), custom_call_target="tpu_custom_call" | custom-call | tf_op jit(solution)/shard_map/pallas_call | solution.py:72
  92.7 2.3 fusion.8
  95.0 133.6 %while.23 = (s32[]{:T(128)}, f32[2048,128]{0,1:T(8,128)}, f32[256,128]{0,1:T(8,128)S(1)}, f32[2048,256]{1,0:T(8,128)S(1)}, f32[256,128]{1,0:T(8,128)}, /*index=5...) while((s32[]{:T(128)}, f32[2048,128]{0,1:T(8,128)}, ...), condition=%wide.region_1.2_spmd, body=%wide.region_0.1_spmd.sunk | while | flops 1309212672 | bytes 17432864 | solution.py:111
  103.1 2.1 fusion.59
  108.9 3.5 %fusion.61 = f32[256,128]{1,0:T(8,128)} fusion(s32[]{:T(128)S(6)} %add.98, f32[1024,256]{1,0:T(8,128)S(1)} %dynamic-slice_bitcast_fusion.2, f32[2048,128]{0,1:T(8,128)} %fusion.59), kind=kOutput, calls=%fused_computation.4.clone.1 | convolution fusion | flops 352321536 | bytes 2097156 | tf_op jit(solution)/shard_map/while/body/eval_jaxpr/dot_general | solution.py:21
  112.3 4.0 %eval_jaxpr.8 = f32[256,256]{1,0:T(8,128)S(1)} custom-call(f32[256,256]{1,0:T(8,128)} %fusion.62.g_ref), custom_call_target="tpu_custom_call" | custom-call | tf_op jit(solution)/shard_map/while/body/eval_jaxpr/pallas_call | solution.py:72
  125.3 2.1 fusion.59
  131.1 3.5 %fusion.61 = f32[256,128]{1,0:T(8,128)} fusion(s32[]{:T(128)S(6)} %add.98, f32[1024,256]{1,0:T(8,128)S(1)} %dynamic-slice_bitcast_fusion.2, f32[2048,128]{0,1:T(8,128)} %fusion.59), kind=kOutput, calls=%fused_computation.4.clone.1 | convolution fusion | flops 352321536 | bytes 2097156 | tf_op jit(solution)/shard_map/while/body/eval_jaxpr/dot_general | solution.py:21
  134.6 4.0 %eval_jaxpr.8 = f32[256,256]{1,0:T(8,128)S(1)} custom-call(f32[256,256]{1,0:T(8,128)} %fusion.62.g_ref), custom_call_target="tpu_custom_call" | custom-call | tf_op jit(solution)/shard_map/while/body/eval_jaxpr/pallas_call | solution.py:72
  147.2 2.1 fusion.59
  153.0 3.5 %fusion.61 = f32[256,128]{1,0:T(8,128)} fusion(s32[]{:T(128)S(6)} %add.98, f32[1024,256]{1,0:T(8,128)S(1)} %dynamic-slice_bitcast_fusion.2, f32[2048,128]{0,1:T(8,128)} %fusion.59), kind=kOutput, calls=%fused_computation.4.clone.1 | convolution fusion | flops 352321536 | bytes 2097156 | tf_op jit(solution)/shard_map/while/body/eval_jaxpr/dot_general | solution.py:21
  156.5 4.0 %eval_jaxpr.8 = f32[256,256]{1,0:T(8,128)S(1)} custom-call(f32[256,256]{1,0:T(8,128)} %fusion.62.g_ref), custom_call_target="tpu_custom_call" | custom-call | tf_op jit(solution)/shard_map/while/body/eval_jaxpr/pallas_call | solution.py:72
  170.1 2.1 fusion.59
  175.9 3.5 %fusion.61 = f32[256,128]{1,0:T(8,128)} fusion(s32[]{:T(128)S(6)} %add.98, f32[1024,256]{1,0:T(8,128)S(1)} %dynamic-slice_bitcast_fusion.2, f32[2048,128]{0,1:T(8,128)} %fusion.59), kind=kOutput, calls=%fused_computation.4.clone.1 | convolution fusion | flops 352321536 | bytes 2097156 | tf_op jit(solution)/shard_map/while/body/eval_jaxpr/dot_general | solution.py:21
  179.3 4.0 %eval_jaxpr.8 = f32[256,256]{1,0:T(8,128)S(1)} custom-call(f32[256,256]{1,0:T(8,128)} %fusion.62.g_ref), custom_call_target="tpu_custom_call" | custom-call | tf_op jit(solution)/shard_map/while/body/eval_jaxpr/pallas_call | solution.py:72
  192.3 2.1 fusion.59
  198.1 3.5 %fusion.61 = f32[256,128]{1,0:T(8,128)} fusion(s32[]{:T(128)S(6)} %add.98, f32[1024,256]{1,0:T(8,128)S(1)} %dynamic-slice_bitcast_fusion.2, f32[2048,128]{0,1:T(8,128)} %fusion.59), kind=kOutput, calls=%fused_computation.4.clone.1 | convolution fusion | flops 352321536 | bytes 2097156 | tf_op jit(solution)/shard_map/while/body/eval_jaxpr/dot_general | solution.py:21
  201.6 4.0 %eval_jaxpr.8 = f32[256,256]{1,0:T(8,128)S(1)} custom-call(f32[256,256]{1,0:T(8,128)} %fusion.62.g_ref), custom_call_target="tpu_custom_call" | custom-call | tf_op jit(solution)/shard_map/while/body/eval_jaxpr/pallas_call | solution.py:72
  214.5 2.1 fusion.59
  220.3 3.5 %fusion.61 = f32[256,128]{1,0:T(8,128)} fusion(s32[]{:T(128)S(6)} %add.98, f32[1024,256]{1,0:T(8,128)S(1)} %dynamic-slice_bitcast_fusion.2, f32[2048,128]{0,1:T(8,128)} %fusion.59), kind=kOutput, calls=%fused_computation.4.clone.1 | convolution fusion | flops 352321536 | bytes 2097156 | tf_op jit(solution)/shard_map/while/body/eval_jaxpr/dot_general | solution.py:21
  223.8 4.0 %eval_jaxpr.8 = f32[256,256]{1,0:T(8,128)S(1)} custom-call(f32[256,256]{1,0:T(8,128)} %fusion.62.g_ref), custom_call_target="tpu_custom_call" | custom-call | tf_op jit(solution)/shard_map/while/body/eval_jaxpr/pallas_call | solution.py:72
  (85 shorter events, 80.5 us)
Async XLA Ops:
  6.5 5.7 %copy-start.2 = (s32[7,1]{0,1:T(1,128)S(1)}, s32[7,1]{0,1:T(1,128)}, u32[]{:S(2)}) copy-start(s32[7,1]{0,1:T(1,128)} %param.7) | copy-start | bytes 88
  6.5 76.4 %all-gather.2.cloned.1.call-start = ((), (), s32[]{:S(2)}) async-start(), calls=%async_computation | async-start | bytes 7569408 | tf_op jit(solution)/shard_map/all_gather | solution.py:87
  10.7 84.3 %collective-permute-start.1 = (f32[256,128]{0,1:T(8,128)S(1)}, f32[256,128]{0,1:T(8,128)S(1)}, u32[]{:S(2)}, u32[]{:S(2)}) collective-permute-start(f32[256,128]{0,1:T(8,128)S(1)} %slice.87), channel_id=1, source_target_pairs={{0,32},{32,64},{64,96},{96,128},{128,160},{160,192},{192,224},{224... | collective-permute-start | bytes 393224 | tf_op jit(solution)/shard_map/ppermute | solution.py:13
  91.5 1.2 copy-start
  98.5 17.8 %collective-permute-start = (f32[256,128]{0,1:T(8,128)}, f32[256,128]{0,1:T(8,128)}, u32[]{:S(2)}, u32[]{:S(2)}) collective-permute-start(f32[256,128]{0,1:T(8,128)} %fusion.60), channel_id=1, source_target_pairs={{0,32},{32,64},{64,96},{96,128},{128,160},{160,192},{192,224},{224... | collective-permute-start | bytes 393224 | tf_op jit(solution)/shard_map/while/body/eval_jaxpr/ppermute | solution.py:13
  120.7 17.9 %collective-permute-start = (f32[256,128]{0,1:T(8,128)}, f32[256,128]{0,1:T(8,128)}, u32[]{:S(2)}, u32[]{:S(2)}) collective-permute-start(f32[256,128]{0,1:T(8,128)} %fusion.60), channel_id=1, source_target_pairs={{0,32},{32,64},{64,96},{96,128},{128,160},{160,192},{192,224},{224... | collective-permute-start | bytes 393224 | tf_op jit(solution)/shard_map/while/body/eval_jaxpr/ppermute | solution.py:13
  142.9 17.6 %collective-permute-start = (f32[256,128]{0,1:T(8,128)}, f32[256,128]{0,1:T(8,128)}, u32[]{:S(2)}, u32[]{:S(2)}) collective-permute-start(f32[256,128]{0,1:T(8,128)} %fusion.60), channel_id=1, source_target_pairs={{0,32},{32,64},{64,96},{96,128},{128,160},{160,192},{192,224},{224... | collective-permute-start | bytes 393224 | tf_op jit(solution)/shard_map/while/body/eval_jaxpr/ppermute | solution.py:13
  164.9 18.5 %collective-permute-start = (f32[256,128]{0,1:T(8,128)}, f32[256,128]{0,1:T(8,128)}, u32[]{:S(2)}, u32[]{:S(2)}) collective-permute-start(f32[256,128]{0,1:T(8,128)} %fusion.60), channel_id=1, source_target_pairs={{0,32},{32,64},{64,96},{96,128},{128,160},{160,192},{192,224},{224... | collective-permute-start | bytes 393224 | tf_op jit(solution)/shard_map/while/body/eval_jaxpr/ppermute | solution.py:13
  187.7 17.9 %collective-permute-start = (f32[256,128]{0,1:T(8,128)}, f32[256,128]{0,1:T(8,128)}, u32[]{:S(2)}, u32[]{:S(2)}) collective-permute-start(f32[256,128]{0,1:T(8,128)} %fusion.60), channel_id=1, source_target_pairs={{0,32},{32,64},{64,96},{96,128},{128,160},{160,192},{192,224},{224... | collective-permute-start | bytes 393224 | tf_op jit(solution)/shard_map/while/body/eval_jaxpr/ppermute | solution.py:13
  209.9 17.9 %collective-permute-start = (f32[256,128]{0,1:T(8,128)}, f32[256,128]{0,1:T(8,128)}, u32[]{:S(2)}, u32[]{:S(2)}) collective-permute-start(f32[256,128]{0,1:T(8,128)} %fusion.60), channel_id=1, source_target_pairs={{0,32},{32,64},{64,96},{96,128},{128,160},{160,192},{192,224},{224... | collective-permute-start | bytes 393224 | tf_op jit(solution)/shard_map/while/body/eval_jaxpr/ppermute | solution.py:13
  232.0 1.3 copy-start.1
Sparse Core Ops, SparseCore 0:
  9.2 73.7 all-gather.1

commit v3 on v2

--- a/solution.py
+++ b/solution.py
@@ -24,34 +24,33 @@
     )
 
 
-def half_inverse(a, size):
+def half_inverses(blocks, size):
     row = lax.broadcasted_iota(jnp.int32, (size, size), 0)
     col = lax.broadcasted_iota(jnp.int32, (size, size), 1)
     eye_mask = row == col
     eye = eye_mask.astype(jnp.float32)
-    diag_col = jnp.sum(jnp.where(eye_mask, a, 0.0), axis=1, keepdims=True)
-    diag_row = jnp.sum(jnp.where(eye_mask, a, 0.0), axis=0, keepdims=True)
     same_base = (row // BASE) == (col // BASE)
-    nilpotent = jnp.where(same_base, a / diag_col, 0.0) - eye
-    product = eye - nilpotent
-    power = nilpotent
+    diag_cols = [jnp.sum(jnp.where(eye_mask, a, 0.0), axis=1, keepdims=True) for a in blocks]
+    diag_rows = [jnp.sum(jnp.where(eye_mask, a, 0.0), axis=0, keepdims=True) for a in blocks]
+    powers = [jnp.where(same_base, a / d, 0.0) - eye for a, d in zip(blocks, diag_cols)]
+    products = [eye - p for p in powers]
     span = 2
     while span < BASE:
-        power = matmul_3x(power, power)
-        product = matmul_3x(product, eye + power)
+        powers = [matmul_3x(p, p) for p in powers]
+        products = [matmul_3x(q, eye + p) for q, p in zip(products, powers)]
         span = span * 2
-    inv = product * (1.0 / diag_row)
+    invs = [q * (1.0 / d) for q, d in zip(products, diag_rows)]
     half = BASE
     while half < size:
         corner_mask = ((row // half) % 2 == 0) & ((col // half) == (row // half) + 1)
-        upper = jnp.where(corner_mask, a, 0.0)
-        inv = inv - matmul_3x(matmul_3x(inv, upper), inv)
+        uppers = [jnp.where(corner_mask, a, 0.0) for a in blocks]
+        invs = [v - matmul_3x(matmul_3x(v, u), v) for v, u in zip(invs, uppers)]
         half = half * 2
-    return inv
+    return invs
 
 
 def tri_inverse_kernel(g_ref, o_ref):
-    size = g_ref.shape[0]
+    ticks, size = g_ref.shape[0], g_ref.shape[1]
     half = size // 2
     row = lax.broadcasted_iota(jnp.int32, (half, half), 0)
     col = lax.broadcasted_iota(jnp.int32, (half, half), 1)
@@ -59,13 +58,18 @@
     def upper_part(x):
         return jnp.where(col > row, x, jnp.where(row == col, x * 0.5, 0.0))
 
-    upper_inv = half_inverse(upper_part(g_ref[:half, :half]), half)
-    lower_inv = half_inverse(upper_part(g_ref[half:, half:]), half)
-    corner = -matmul_3x(matmul_3x(upper_inv, g_ref[:half, half:]), lower_inv)
-    o_ref[:half, :half] = upper_inv
-    o_ref[:half, half:] = corner
-    o_ref[half:, :half] = jnp.zeros((half, half), jnp.float32)
-    o_ref[half:, half:] = lower_inv
+    blocks = []
+    for t in range(ticks):
+        blocks.append(upper_part(g_ref[t, :half, :half]))
+        blocks.append(upper_part(g_ref[t, half:, half:]))
+    invs = half_inverses(blocks, half)
+    for t in range(ticks):
+        upper_inv, lower_inv = invs[2 * t], invs[2 * t + 1]
+        corner = -matmul_3x(matmul_3x(upper_inv, g_ref[t, :half, half:]), lower_inv)
+        o_ref[t, :half, :half] = upper_inv
+        o_ref[t, :half, half:] = corner
+        o_ref[t, half:, :half] = jnp.zeros((half, half), jnp.float32)
+        o_ref[t, half:, half:] = lower_inv
 
 
 def tri_inverse(gram):
@@ -85,11 +89,13 @@
     rows_here = eigvecs.shape[0]
     ticks = reflectors.shape[0]
     gathered = lax.all_gather(reflectors, "vecs", axis=1, tiled=True)
+    grams = jnp.einsum("tkr,tks->trs", gathered, gathered, precision=lax.Precision.HIGH, preferred_element_type=jnp.float32)
+    solves = tri_inverse(grams)
     first_rows = offsets[:, 0]
 
     def prepare(step, block):
         reflector = lax.dynamic_index_in_dim(gathered, step, 0, keepdims=False)
-        solve = tri_inverse(project_onto(reflector, reflector))
+        solve = lax.dynamic_index_in_dim(solves, step, 0, keepdims=False)
         placed = placed_reflector(reflector, first_rows[step], rows_here)
         own_part = lax.optimization_barrier(project_onto(placed[H:], block[: rows_here - H]))
         return placed, own_part, solve

time: 245 us -> 226 us (0.922)
  Pallas kernels: 27.7 us -> 8.38 us
  local copies, waits for them, and re-layouts: 36.5 us -> 43 us
  matrix products: 74.3 us -> 68.2 us
    pallas_call x7 -> x1, Pallas kernels: 27.7 us -> 8.38 us  [tri_inverse(): pl.pallas_call(tri_inverse_kernel, out_shape=jax.ShapeDtypeStruct(gram.sh...]
    dot_general x21 -> x14, matrix products: 45.3 us -> 31.8 us  [project_onto(): lax.dot_general(left, right, (((left.ndim - 2,), (right.ndim - 2,)), ((),...]
    dot_general x0 -> x1, matrix products: none -> 7.43 us  [shards(): jnp.einsum('tkr,tks->trs', gathered, gathered, precision=lax.Precision.HI...]
    squeeze x0 -> x7, local copies, waits for them, and re-layouts: none -> 6.77 us  [prepare(): solve = lax.dynamic_index_in_dim(solves, step, 0, keepdims=False)]
  transfers between devices with their start and end apart: 8 -> 8, of which waited for: 1 -> 1; matrix products, arithmetic and copies ran while one was open for 32% -> 35% of each run, Pallas kernels for 11% -> 4%
where the time goes in v3:
time: 226 us; the launch traced here: 223 us
  waiting for transfers between devices  71.3 us (32%)
  matrix products  68.2 us (30%)
  local copies, waits for them, and re-layouts  43 us (19%)
  between operations  13.5 us (6%)
  starting transfers between devices  10.7 us (5%)
  Pallas kernels  8.38 us (4%)
  loops' own time  8.14 us (4%)
    all_gather x1, waiting for transfers between devices, shards(): gathered = lax.all_gather(reflectors, 'vecs', axis=1, tiled=True)  70.5 us
    dot_general x14, matrix products, project_onto(): lax.dot_general(left, right, (((left.ndim - 2,), (right.ndim - 2,)), ((),...  31.8 us
    dot_general x20, matrix products, matmul_3x(): jnp.matmul(left, right, precision=lax.Precision.HIGH, preferred_element_t...  29 us
    ppermute x7, starting transfers between devices, passed_along(): return lax.ppermute(x, axis, [(i, (i + by) % size) for i in range(size)])  10.7 us
    squeeze x7, local copies, waits for them, and re-layouts, prepare(): reflector = lax.dynamic_index_in_dim(gathered, step, 0, keepdims=False)  9.19 us
    pallas_call x1, Pallas kernels, tri_inverse(): pl.pallas_call(tri_inverse_kernel, out_shape=jax.ShapeDtypeStruct(gram.sh...  8.38 us
    another operation x1, loops' own time, shards(): carry = lax.fori_loop(0, ticks - 1, tick, carry)  8.14 us
    slice x7, local copies, waits for them, and re-layouts, finish(): return (weights, jnp.concatenate([incoming, block[:rows_here - H]], axis=0))  7.49 us
  transfers between devices with their start and end apart: 8, of which 1 were waited for; matrix products, arithmetic and copies ran while one was open for 35% of the time, Pallas kernels for 4%

profile of v3, /device:TPU:8, one launch (start us, length us, event | category | flops | bytes accessed | tf_op | source)
XLA Modules:
  0.0 223.2 jit_solution(13076191314523897905)
XLA Ops:
  7.3 2.6 %copy.5 = f32[2048,128]{0,1:T(8,128)} copy(f32[2048,128]{1,0:T(8,128)} %param.5) | data formatting | bytes 2097152 | tf_op jit(solution)/shard_map/while | solution.py:117
  12.5 70.5 %all-gather.2.cloned.1.call-done = f32[7,1024,256]{2,1,0:T(8,128)} async-done(((f32[7,32,256]{2,1,0:T(8,128)}), f32[7,1024,256]{2,1,0:T(8,128)}) %all-gather.2.cloned.1.call-update) | async-done | bytes 7340048 | tf_op jit(solution)/shard_map/all_gather | solution.py:91
  85.1 2.3 %fusion.8 = f32[256,128]{1,0:T(8,128)} fusion(s32[]{:T(128)S(6)} %add.89, f32[1024,256]{1,0:T(8,128)S(1)} %slice_bitcast_fusion, f32[2048,128]{1,0:T(8,128)S(1)} %copy-done.1), kind=kOutput, calls=%fused_computation.18 | convolution fusion | flops 352321536 | bytes 2097156 | tf_op jit(solution)/shard_map/dot_general | solution.py:21
  87.4 7.4 %fusion.17.g_ref = f32[7,256,256]{2,1,0:T(8,128)} fusion(f32[7,1024,256]{2,1,0:T(8,128)S(1)} %copy-done), kind=kOutput, calls=%fused_computation.29 | convolution fusion | flops 2818572288 | bytes 9175040 | tf_op jit(solution)/shard_map/tkr,tks->trs/dot_general | solution.py:92
  94.9 8.4 %shard_map.37 = f32[7,256,256]{2,1,0:T(8,128)} custom-call(f32[7,256,256]{2,1,0:T(8,128)} %fusion.17.g_ref), custom_call_target="tpu_custom_call" | custom-call | tf_op jit(solution)/shard_map/pallas_call | solution.py:76
  104.2 105.5 %while.23 = (s32[]{:T(128)}, f32[2048,128]{0,1:T(8,128)}, f32[256,128]{0,1:T(8,128)S(1)}, f32[2048,256]{1,0:T(8,128)S(1)}, f32[256,128]{1,0:T(8,128)}, /*index=5...) while((s32[]{:T(128)}, f32[2048,128]{0,1:T(8,128)}, ...), condition=%wide.region_1.2_spmd, body=%wide.region_0.1_spmd.sunk | while | flops 906559488 | bytes 16646445 | solution.py:117
  105.8 1.9 fusion.54
  112.3 2.1 fusion.53
  116.4 3.5 %fusion.55 = f32[256,128]{1,0:T(8,128)} fusion(s32[]{:T(128)S(6)} %add.102, f32[1024,256]{1,0:T(8,128)S(1)} %dynamic-slice_bitcast_fusion.4, f32[2048,128]{0,1:T(8,128)} %fusion.53), kind=kOutput, calls=%fused_computation.4.clone.1 | convolution fusion | flops 352321536 | bytes 2097156 | tf_op jit(solution)/shard_map/while/body/eval_jaxpr/dot_general | solution.py:21
  123.3 1.9 fusion.54
  129.8 2.1 fusion.53
  133.9 3.5 %fusion.55 = f32[256,128]{1,0:T(8,128)} fusion(s32[]{:T(128)S(6)} %add.102, f32[1024,256]{1,0:T(8,128)S(1)} %dynamic-slice_bitcast_fusion.4, f32[2048,128]{0,1:T(8,128)} %fusion.53), kind=kOutput, calls=%fused_computation.4.clone.1 | convolution fusion | flops 352321536 | bytes 2097156 | tf_op jit(solution)/shard_map/while/body/eval_jaxpr/dot_general | solution.py:21
  140.9 1.9 fusion.54
  147.1 2.1 fusion.53
  151.2 3.5 %fusion.55 = f32[256,128]{1,0:T(8,128)} fusion(s32[]{:T(128)S(6)} %add.102, f32[1024,256]{1,0:T(8,128)S(1)} %dynamic-slice_bitcast_fusion.4, f32[2048,128]{0,1:T(8,128)} %fusion.53), kind=kOutput, calls=%fused_computation.4.clone.1 | convolution fusion | flops 352321536 | bytes 2097156 | tf_op jit(solution)/shard_map/while/body/eval_jaxpr/dot_general | solution.py:21
  160.0 2.1 collective-permute-start
  165.2 2.1 fusion.53
  169.3 3.5 %fusion.55 = f32[256,128]{1,0:T(8,128)} fusion(s32[]{:T(128)S(6)} %add.102, f32[1024,256]{1,0:T(8,128)S(1)} %dynamic-slice_bitcast_fusion.4, f32[2048,128]{0,1:T(8,128)} %fusion.53), kind=kOutput, calls=%fused_computation.4.clone.1 | convolution fusion | flops 352321536 | bytes 2097156 | tf_op jit(solution)/shard_map/while/body/eval_jaxpr/dot_general | solution.py:21
  176.3 1.9 fusion.54
  182.7 2.1 fusion.53
  186.8 3.5 %fusion.55 = f32[256,128]{1,0:T(8,128)} fusion(s32[]{:T(128)S(6)} %add.102, f32[1024,256]{1,0:T(8,128)S(1)} %dynamic-slice_bitcast_fusion.4, f32[2048,128]{0,1:T(8,128)} %fusion.53), kind=kOutput, calls=%fused_computation.4.clone.1 | convolution fusion | flops 352321536 | bytes 2097156 | tf_op jit(solution)/shard_map/while/body/eval_jaxpr/dot_general | solution.py:21
  200.2 2.1 fusion.53
  204.3 3.5 %fusion.55 = f32[256,128]{1,0:T(8,128)} fusion(s32[]{:T(128)S(6)} %add.102, f32[1024,256]{1,0:T(8,128)S(1)} %dynamic-slice_bitcast_fusion.4, f32[2048,128]{0,1:T(8,128)} %fusion.53), kind=kOutput, calls=%fused_computation.4.clone.1 | convolution fusion | flops 352321536 | bytes 2097156 | tf_op jit(solution)/shard_map/while/body/eval_jaxpr/dot_general | solution.py:21
  214.4 2.0 convolution_subtract_fusion
  (82 shorter events, 65.2 us)
Async XLA Ops:
  6.5 5.8 %copy-start.3 = (s32[7,1]{0,1:T(1,128)S(1)}, s32[7,1]{0,1:T(1,128)}, u32[]{:S(2)}) copy-start(s32[7,1]{0,1:T(1,128)} %param.7) | copy-start | bytes 88
  6.5 76.4 %all-gather.2.cloned.1.call-start = ((), (), s32[]{:S(2)}) async-start(), calls=%async_computation | async-start | bytes 7569408 | tf_op jit(solution)/shard_map/all_gather | solution.py:91
  7.3 77.9 %copy-start.1 = (f32[2048,128]{1,0:T(8,128)S(1)}, f32[2048,128]{1,0:T(8,128)}, u32[]{:S(2)}) copy-start(f32[2048,128]{1,0:T(8,128)} %param.5) | copy-start | bytes 3145732
  10.8 93.4 %collective-permute-start.1 = (f32[256,128]{0,1:T(8,128)S(1)}, f32[256,128]{0,1:T(8,128)S(1)}, u32[]{:S(2)}, u32[]{:S(2)}) collective-permute-start(f32[256,128]{0,1:T(8,128)S(1)} %slice.88), channel_id=1, source_target_pairs={{0,32},{32,64},{64,96},{96,128},{128,160},{160,192},{192,224},{224... | collective-permute-start | bytes 393224 | tf_op jit(solution)/shard_map/ppermute | solution.py:13
  83.0 4.4 %copy-start = (f32[7,1024,256]{2,1,0:T(8,128)S(1)}, f32[7,1024,256]{2,1,0:T(8,128)}, u32[]{:S(2)}) copy-start(f32[7,1024,256]{2,1,0:T(8,128)} %all-gather.2.cloned.1.call-done) | copy-start | bytes 22020100
  107.7 13.2 %collective-permute-start = (f32[256,128]{0,1:T(8,128)}, f32[256,128]{0,1:T(8,128)}, u32[]{:S(2)}, u32[]{:S(2)}) collective-permute-start(f32[256,128]{0,1:T(8,128)} %fusion.54), channel_id=1, source_target_pairs={{0,32},{32,64},{64,96},{96,128},{128,160},{160,192},{192,224},{224... | collective-permute-start | bytes 393224 | tf_op jit(solution)/shard_map/while/body/eval_jaxpr/ppermute | solution.py:13
  125.2 13.2 %collective-permute-start = (f32[256,128]{0,1:T(8,128)}, f32[256,128]{0,1:T(8,128)}, u32[]{:S(2)}, u32[]{:S(2)}) collective-permute-start(f32[256,128]{0,1:T(8,128)} %fusion.54), channel_id=1, source_target_pairs={{0,32},{32,64},{64,96},{96,128},{128,160},{160,192},{192,224},{224... | collective-permute-start | bytes 393224 | tf_op jit(solution)/shard_map/while/body/eval_jaxpr/ppermute | solution.py:13
  142.7 12.9 %collective-permute-start = (f32[256,128]{0,1:T(8,128)}, f32[256,128]{0,1:T(8,128)}, u32[]{:S(2)}, u32[]{:S(2)}) collective-permute-start(f32[256,128]{0,1:T(8,128)} %fusion.54), channel_id=1, source_target_pairs={{0,32},{32,64},{64,96},{96,128},{128,160},{160,192},{192,224},{224... | collective-permute-start | bytes 393224 | tf_op jit(solution)/shard_map/while/body/eval_jaxpr/ppermute | solution.py:13
  160.0 13.8 %collective-permute-start = (f32[256,128]{0,1:T(8,128)}, f32[256,128]{0,1:T(8,128)}, u32[]{:S(2)}, u32[]{:S(2)}) collective-permute-start(f32[256,128]{0,1:T(8,128)} %fusion.54), channel_id=1, source_target_pairs={{0,32},{32,64},{64,96},{96,128},{128,160},{160,192},{192,224},{224... | collective-permute-start | bytes 393224 | tf_op jit(solution)/shard_map/while/body/eval_jaxpr/ppermute | solution.py:13
  178.1 13.1 %collective-permute-start = (f32[256,128]{0,1:T(8,128)}, f32[256,128]{0,1:T(8,128)}, u32[]{:S(2)}, u32[]{:S(2)}) collective-permute-start(f32[256,128]{0,1:T(8,128)} %fusion.54), channel_id=1, source_target_pairs={{0,32},{32,64},{64,96},{96,128},{128,160},{160,192},{192,224},{224... | collective-permute-start | bytes 393224 | tf_op jit(solution)/shard_map/while/body/eval_jaxpr/ppermute | solution.py:13
  195.6 13.1 %collective-permute-start = (f32[256,128]{0,1:T(8,128)}, f32[256,128]{0,1:T(8,128)}, u32[]{:S(2)}, u32[]{:S(2)}) collective-permute-start(f32[256,128]{0,1:T(8,128)} %fusion.54), channel_id=1, source_target_pairs={{0,32},{32,64},{64,96},{96,128},{128,160},{160,192},{192,224},{224... | collective-permute-start | bytes 393224 | tf_op jit(solution)/shard_map/while/body/eval_jaxpr/ppermute | solution.py:13
  211.5 2.9 %copy-start.2 = (f32[256,128]{1,0:T(8,128)S(1)}, f32[256,128]{1,0:T(8,128)}, u32[]{:S(2)}) copy-start(f32[256,128]{1,0:T(8,128)} %copy.7) | copy-start | bytes 393220
Sparse Core Ops, SparseCore 0:
  9.2 73.7 all-gather.1
